TPU v7x, 256 devices: a whole 4x4x8 slice. The times are simulated.
256 devices in a mesh: dp: 16 (over y, x), section: 2 (over core), tensor: 8 (over z).
Axes of the slice: x: 4, y: 4, z: 8, core: 2. Of those that a mesh axis runs over, the one named last changes fastest.
Arguments:
- tokens: bfloat16 [2048, 16384], P('dp'), may hold values from -9 to 9
- order: int32 [2048], replicated, may hold values from 0 to 2047, as said below
- segments: int32 [2048], replicated, may hold values from 0 to 1, as said below
- gain: float32 [2, 16384], P('section', 'dp'), may hold values from 0.1 to 1.9
- w_query: bfloat16 [2, 16384, 8192], P('section', 'dp', 'tensor'), may hold values from -0.046875 to 0.046875
- key_value_weight: bfloat16 [2, 16384, 8, 256], P('section', 'dp', 'tensor'), may hold values from -0.046875 to 0.046875
- w_out: bfloat16 [2, 8192, 16384], P('section', 'tensor', 'dp'), may hold values from -0.0625 to 0.0625
Outputs:
- layer_out: bfloat16 [2048, 16384], P('section', 'dp')
Inputs may be any that keep to these rules, and one draw needn't show every extreme that they name: A permutation that moves whole sentences: the rows of one sentence (a run of equal segments within a block of 32 rows) come from consecutive entry rows in order. `segments`: within each block of 32 rows the sentence numbers do not fall and each of 0 to 1 appears.
All inputs are finite; a program needn't handle non-finite values.
Results may differ from a plain program's by a relative error of at most 0.022.
Values may be sent and summed in bfloat16 or wider, within the bound.
No kernel may reach another device: no remote copies, remote signals or barrier semaphores. Data moves between devices by JAX's collectives and lax.ppermute only.
A program may use at most 64 MiB of HBM per device.

v0:
```python
import math
import jax
import jax.numpy as jnp
from jax import lax
from jax.sharding import PartitionSpec as P

MODEL_WIDTH = 16384
KEYVALUE_HEADS = 8
QUERY_HEADS = 64
MICRO_TOKENS = 32
M = 4
norm_epsilon = 1e-05


def passed_along(array, axis, by):
    count = lax.axis_size(axis)
    return lax.ppermute(array, axis, [(i, (i + by) % count) for i in range(count)])


def causal_block_attend(query_rows, key_value_rows, sentence_segment_rows, query_group_width):
    row_count = query_rows.shape[0]
    kv_heads = key_value_rows.shape[1]
    head_size = key_value_rows.shape[2] // 2
    query_head_rows = query_rows.reshape(row_count, kv_heads, query_group_width, head_size)
    key_heads = key_value_rows[:, :, :head_size]
    value_heads = key_value_rows[:, :, head_size:]
    scores = jnp.einsum(
        "qkgd,skd->kgqs", query_head_rows, key_heads, preferred_element_type=jnp.float32
    ) / math.sqrt(head_size)
    position = jnp.arange(row_count)
    allowed = (sentence_segment_rows[:, None] == sentence_segment_rows[None, :]) & (
        position[None, :] <= position[:, None]
    )
    raw_weights = jnp.where(allowed[None, None], jnp.exp(scores), 0.0)
    totals = jnp.sum(raw_weights, axis=-1, keepdims=True)
    probs = (raw_weights / totals).astype(jnp.bfloat16)
    attended_rows = jnp.einsum(
        "kgqs,skd->qkgd", probs, value_heads, preferred_element_type=jnp.float32
    )
    return attended_rows.astype(jnp.bfloat16).reshape(
        row_count, kv_heads * query_group_width * head_size
    )


def section_layer(
    hidden, sentence_segment_rows, gain_row, query_weight, key_value_matrix, out_weight
):
    slice_width = hidden.shape[1]
    own_rows = sentence_segment_rows.shape[0]
    own_start = lax.axis_index("dp") * own_rows
    widened = hidden.astype(jnp.float32)
    normed_rows = (widened * gain_row[None, :]).astype(jnp.bfloat16)
    query_terms = jnp.dot(normed_rows, query_weight, preferred_element_type=jnp.float32)
    keyval_terms = jnp.dot(
        normed_rows, key_value_matrix.reshape(slice_width, -1), preferred_element_type=jnp.float32
    )
    square_terms = jnp.sum(widened * widened, axis=1)
    all_squares = lax.psum(square_terms, "dp")
    own_squares = lax.dynamic_slice_in_dim(all_squares, own_start, own_rows)
    query_sums, keyval_sums = (
        lax.psum_scatter(
            query_terms.astype(jnp.bfloat16), "dp", scatter_dimension=0, tiled=True
        ).astype(jnp.float32),
        lax.psum_scatter(
            keyval_terms.astype(jnp.bfloat16), "dp", scatter_dimension=0, tiled=True
        ).astype(jnp.float32),
    )
    root_mean_square = jnp.sqrt(own_squares / MODEL_WIDTH + norm_epsilon)
    query_rows = (query_sums / root_mean_square[:, None]).astype(jnp.bfloat16)
    kv_heads = key_value_matrix.shape[1]
    key_value_rows = (
        (keyval_sums / root_mean_square[:, None])
        .astype(jnp.bfloat16)
        .reshape(own_rows, kv_heads, key_value_matrix.shape[2])
    )
    attended_rows = causal_block_attend(
        query_rows, key_value_rows, sentence_segment_rows, QUERY_HEADS // KEYVALUE_HEADS
    )
    head_terms = jnp.dot(
        lax.all_gather(attended_rows, "dp", axis=0, tiled=True),
        out_weight,
        preferred_element_type=jnp.float32,
    )
    head_total = lax.psum(head_terms.astype(jnp.bfloat16), "tensor").astype(jnp.float32)
    return (widened + head_total).astype(jnp.bfloat16)


def on_device(tokens, order, segments, gain, w_query, key_value_weight, w_out):
    spread = lax.all_to_all(tokens, "dp", split_axis=1, concat_axis=0, tiled=True)
    arranged = jnp.take(spread, order, axis=0)
    group_count = lax.axis_size("dp")
    rows_all = group_count * MICRO_TOKENS
    section_index = lax.axis_index("section")
    group_index = lax.axis_index("dp")
    gain_row = gain[0]
    query_weight = w_query[0]
    key_value_matrix = key_value_weight[0]
    out_weight = w_out[0]
    received = jnp.zeros((rows_all, arranged.shape[1]), jnp.bfloat16)
    inbox = []
    results = []
    for turn_index in range(M + 1):
        if turn_index < M:
            fresh = arranged[turn_index * rows_all : (turn_index + 1) * rows_all]
        else:
            fresh = jnp.zeros_like(received)
        micro_index = jnp.where(
            section_index == 0, min(turn_index, M - 1), max(turn_index - 1, 0)
        ).astype(jnp.int32)
        sentence_segment_rows = lax.dynamic_slice_in_dim(
            segments, micro_index * rows_all + group_index * MICRO_TOKENS, MICRO_TOKENS
        )
        layer_input = jnp.where(section_index == 0, fresh, received)
        layer_output = section_layer(
            layer_input, sentence_segment_rows, gain_row, query_weight, key_value_matrix, out_weight
        )
        inbox.append(received)
        results.append(layer_output)
        if turn_index < M:
            received = passed_along(layer_output, "section", 1)
    half_count = M // 2
    from_back = jnp.concatenate(
        [inbox[index_value + 2] for index_value in range(half_count)], axis=0
    )
    kept_here = jnp.concatenate(
        [results[index_value + 1] for index_value in range(half_count, M)], axis=0
    )
    return jnp.where(section_index == 0, from_back, kept_here)


def solution(mesh):
    placed = (
        P("dp", None),
        P(),
        P(),
        P("section", "dp"),
        P("section", "dp", "tensor"),
        P("section", "dp", "tensor", None),
        P("section", "tensor", "dp"),
    )
    return jax.shard_map(
        on_device, mesh=mesh, in_specs=placed, out_specs=P("section", "dp"), check_vma=False
    )
```

profile of v0, /device:TPU:2, one launch (start us, length us, event | category | flops | bytes accessed | tf_op | source)
XLA Modules:
  0.0 1587.2 jit_solution(1069376487911914419)
XLA Ops:
  6.5 4.9 copy.87
  11.5 7.6 all-to-all-start
  19.2 59.1 %all-to-all-done = bf16[128,16,1024]{2,0,1:T(8,128)(2,1)} async-done(((bf16[128,16,1024]{2,0,1:T(8,128)(2,1)}), bf16[128,16,1024]{2,0,1:T(8,128)(2,1)}, u32[]{:S(2)}, u32[]{:S(2)}) %all-to-all-start) | async-done | bytes 4194336 | tf_op jit(solution)/shard_map/all_to_all | solution.py:89
  78.3 13.7 gather_fusion
  103.8 39.7 %psum.70 = f32[512]{0:T(512)S(1)} all-reduce(f32[512]{0:T(512)S(1)} %fusion.1), channel_id=1, replica_groups=mesh['dp'=16,'section'=2,'tensor'=8] {'dp'}, use_global_device_ids=true, to_apply=%region_2.3 | all-reduce | flops 512 | bytes 4096 | tf_op jit(solution)/shard_map/psum | solution.py:58
  143.6 36.6 %reduce-scatter.11.cloned.1.call-done = bf16[32,256]{1,0:T(8,128)(2,1)} async-done(((bf16[512,256]{1,0:T(8,128)(2,1)}), bf16[32,256]{1,0:T(8,128)(2,1)}) %reduce-scatter.11.cloned.1.call-update) | async-done | bytes 16400 | tf_op jit(solution)/shard_map/reduce_scatter | solution.py:64
  181.0 81.3 %reduce-scatter.13.cloned.1.call-done = bf16[32,1024]{1,0:T(8,128)(2,1)} async-done(((bf16[512,1024]{1,0:T(8,128)(2,1)}), bf16[32,1024]{1,0:T(8,128)(2,1)}) %reduce-scatter.13.cloned.1.call-update) | async-done | bytes 65552 | tf_op jit(solution)/shard_map/reduce_scatter | solution.py:61
  264.4 47.2 %all-gather.6.cloned.1.call-done = bf16[512,1024]{1,0:T(8,128)(2,1)} async-done(((bf16[32,1024]{1,0:T(8,128)(2,1)}), bf16[512,1024]{1,0:T(8,128)(2,1)}) %all-gather.6.cloned.1.call-update) | async-done | bytes 1048592 | tf_op jit(solution)/shard_map/all_gather | solution.py:80
  315.8 75.8 %all-reduce.6.cloned.1.call-done = bf16[512,1024]{1,0:T(8,128)(2,1)} async-done(((bf16[512,1024]{1,0:T(8,128)(2,1)}), bf16[512,1024]{1,0:T(8,128)(2,1)}) %all-reduce.6.cloned.1.call-update) | async-done | bytes 1048592 | tf_op jit(solution)/shard_map/psum | solution.py:84
  401.6 36.4 %psum.72 = f32[512]{0:T(512)S(1)} all-reduce(f32[512]{0:T(512)S(1)} %get-tuple-element.9), channel_id=1, replica_groups=mesh['dp'=16,'section'=2,'tensor'=8] {'dp'}, use_global_device_ids=true, to_apply=%region_8.9 | all-reduce | flops 512 | bytes 4096 | tf_op jit(solution)/shard_map/psum | solution.py:58
  438.1 37.8 %reduce-scatter.15.cloned.1.call-done = bf16[32,256]{1,0:T(8,128)(2,1)} async-done(((bf16[512,256]{1,0:T(8,128)(2,1)}), bf16[32,256]{1,0:T(8,128)(2,1)}) %reduce-scatter.15.cloned.1.call-update) | async-done | bytes 16400 | tf_op jit(solution)/shard_map/reduce_scatter | solution.py:64
  476.6 80.9 %reduce-scatter.17.cloned.1.call-done = bf16[32,1024]{1,0:T(8,128)(2,1)} async-done(((bf16[512,1024]{1,0:T(8,128)(2,1)}), bf16[32,1024]{1,0:T(8,128)(2,1)}) %reduce-scatter.17.cloned.1.call-update) | async-done | bytes 65552 | tf_op jit(solution)/shard_map/reduce_scatter | solution.py:61
  559.7 47.2 %all-gather.8.cloned.1.call-done = bf16[512,1024]{1,0:T(8,128)(2,1)} async-done(((bf16[32,1024]{1,0:T(8,128)(2,1)}), bf16[512,1024]{1,0:T(8,128)(2,1)}) %all-gather.8.cloned.1.call-update) | async-done | bytes 1048592 | tf_op jit(solution)/shard_map/all_gather | solution.py:80
  611.1 75.8 %all-reduce.8.cloned.1.call-done = bf16[512,1024]{1,0:T(8,128)(2,1)} async-done(((bf16[512,1024]{1,0:T(8,128)(2,1)}), bf16[512,1024]{1,0:T(8,128)(2,1)}) %all-reduce.8.cloned.1.call-update) | async-done | bytes 1048592 | tf_op jit(solution)/shard_map/psum | solution.py:84
  699.0 36.4 %psum.74 = f32[512]{0:T(512)S(1)} all-reduce(f32[512]{0:T(512)S(1)} %get-tuple-element.7), channel_id=1, replica_groups=mesh['dp'=16,'section'=2,'tensor'=8] {'dp'}, use_global_device_ids=true, to_apply=%region_14.15 | all-reduce | flops 512 | bytes 4096 | tf_op jit(solution)/shard_map/psum | solution.py:58
  735.5 36.5 %reduce-scatter.19.cloned.1.call-done = bf16[32,256]{1,0:T(8,128)(2,1)} async-done(((bf16[512,256]{1,0:T(8,128)(2,1)}), bf16[32,256]{1,0:T(8,128)(2,1)}) %reduce-scatter.19.cloned.1.call-update) | async-done | bytes 16400 | tf_op jit(solution)/shard_map/reduce_scatter | solution.py:64
  772.7 81.0 %reduce-scatter.21.cloned.1.call-done = bf16[32,1024]{1,0:T(8,128)(2,1)} async-done(((bf16[512,1024]{1,0:T(8,128)(2,1)}), bf16[32,1024]{1,0:T(8,128)(2,1)}) %reduce-scatter.21.cloned.1.call-update) | async-done | bytes 65552 | tf_op jit(solution)/shard_map/reduce_scatter | solution.py:61
  855.9 47.2 %all-gather.10.cloned.1.call-done = bf16[512,1024]{1,0:T(8,128)(2,1)} async-done(((bf16[32,1024]{1,0:T(8,128)(2,1)}), bf16[512,1024]{1,0:T(8,128)(2,1)}) %all-gather.10.cloned.1.call-update) | async-done | bytes 1048592 | tf_op jit(solution)/shard_map/all_gather | solution.py:80
  903.1 4.2 fusion.56
  907.4 75.8 %all-reduce.10.cloned.1.call-done = bf16[512,1024]{1,0:T(8,128)(2,1)} async-done(((bf16[512,1024]{1,0:T(8,128)(2,1)}), bf16[512,1024]{1,0:T(8,128)(2,1)}) %all-reduce.10.cloned.1.call-update) | async-done | bytes 1048592 | tf_op jit(solution)/shard_map/psum | solution.py:84
  996.5 36.4 %psum.76 = f32[512]{0:T(512)S(1)} all-reduce(f32[512]{0:T(512)S(1)} %get-tuple-element.5), channel_id=1, replica_groups=mesh['dp'=16,'section'=2,'tensor'=8] {'dp'}, use_global_device_ids=true, to_apply=%region_20.21 | all-reduce | flops 512 | bytes 4096 | tf_op jit(solution)/shard_map/psum | solution.py:58
  1032.9 36.5 %reduce-scatter.23.cloned.1.call-done = bf16[32,256]{1,0:T(8,128)(2,1)} async-done(((bf16[512,256]{1,0:T(8,128)(2,1)}), bf16[32,256]{1,0:T(8,128)(2,1)}) %reduce-scatter.23.cloned.1.call-update) | async-done | bytes 16400 | tf_op jit(solution)/shard_map/reduce_scatter | solution.py:64
  1070.2 80.9 %reduce-scatter.25.cloned.1.call-done = bf16[32,1024]{1,0:T(8,128)(2,1)} async-done(((bf16[512,1024]{1,0:T(8,128)(2,1)}), bf16[32,1024]{1,0:T(8,128)(2,1)}) %reduce-scatter.25.cloned.1.call-update) | async-done | bytes 65552 | tf_op jit(solution)/shard_map/reduce_scatter | solution.py:61
  1153.2 47.1 %all-gather.12.cloned.1.call-done = bf16[512,1024]{1,0:T(8,128)(2,1)} async-done(((bf16[32,1024]{1,0:T(8,128)(2,1)}), bf16[512,1024]{1,0:T(8,128)(2,1)}) %all-gather.12.cloned.1.call-update) | async-done | bytes 1048592 | tf_op jit(solution)/shard_map/all_gather | solution.py:80
  1200.3 4.2 fusion.59
  1204.5 75.8 %all-reduce.12.cloned.1.call-done = bf16[512,1024]{1,0:T(8,128)(2,1)} async-done(((bf16[512,1024]{1,0:T(8,128)(2,1)}), bf16[512,1024]{1,0:T(8,128)(2,1)}) %all-reduce.12.cloned.1.call-update) | async-done | bytes 1048592 | tf_op jit(solution)/shard_map/psum | solution.py:84
  1291.0 36.4 %psum.78 = f32[512]{0:T(512)S(1)} all-reduce(f32[512]{0:T(512)S(1)} %fusion.13), channel_id=1, replica_groups=mesh['dp'=16,'section'=2,'tensor'=8] {'dp'}, use_global_device_ids=true, to_apply=%region_26.27 | all-reduce | flops 512 | bytes 4096 | tf_op jit(solution)/shard_map/psum | solution.py:58
  1327.5 37.4 %reduce-scatter.27.cloned.1.call-done = bf16[32,256]{1,0:T(8,128)(2,1)} async-done(((bf16[512,256]{1,0:T(8,128)(2,1)}), bf16[32,256]{1,0:T(8,128)(2,1)}) %reduce-scatter.27.cloned.1.call-update) | async-done | bytes 16400 | tf_op jit(solution)/shard_map/reduce_scatter | solution.py:64
  1365.7 81.0 %reduce-scatter.29.cloned.1.call-done = bf16[32,1024]{1,0:T(8,128)(2,1)} async-done(((bf16[512,1024]{1,0:T(8,128)(2,1)}), bf16[32,1024]{1,0:T(8,128)(2,1)}) %reduce-scatter.29.cloned.1.call-update) | async-done | bytes 65552 | tf_op jit(solution)/shard_map/reduce_scatter | solution.py:61
  1449.0 47.0 %all-gather.14.cloned.1.call-done = bf16[512,1024]{1,0:T(8,128)(2,1)} async-done(((bf16[32,1024]{1,0:T(8,128)(2,1)}), bf16[512,1024]{1,0:T(8,128)(2,1)}) %all-gather.14.cloned.1.call-update) | async-done | bytes 1048592 | tf_op jit(solution)/shard_map/all_gather | solution.py:80
  1496.0 4.2 fusion.62
  1500.2 75.9 %all-reduce.14.cloned.1.call-done = bf16[512,1024]{1,0:T(8,128)(2,1)} async-done(((bf16[512,1024]{1,0:T(8,128)(2,1)}), bf16[512,1024]{1,0:T(8,128)(2,1)}) %all-reduce.14.cloned.1.call-update) | async-done | bytes 1048592 | tf_op jit(solution)/shard_map/psum | solution.py:84
  (142 shorter events, 85.3 us)
Async XLA Ops:
  6.5 91.2 %copy-start = (bf16[1,1024,1024]{2,1,0:T(8,128)(2,1)S(1)}, bf16[1,1024,1024]{2,1,0:T(8,128)(2,1)}, u32[]{:S(2)}) copy-start(bf16[1,1024,1024]{2,1,0:T(8,128)(2,1)} %param.11) | copy-start | bytes 6291460
  11.5 7.7 copy-start.9
  11.5 66.8 %all-to-all-start = ((bf16[128,16,1024]{2,0,1:T(8,128)(2,1)}), bf16[128,16,1024]{2,0,1:T(8,128)(2,1)}, u32[]{:S(2)}, u32[]{:S(2)}) async-start(bf16[128,16,1024]{2,0,1:T(8,128)(2,1)} %bitcast.266), calls=%async_computation | async-start | bytes 8388608 | tf_op jit(solution)/shard_map/all_to_all | solution.py:89
  19.1 161.1 %reduce-scatter.11.cloned.1.call-start = ((), (), s32[]{:S(2)}) async-start(), calls=%async_computation.11 | async-start | bytes 278528 | tf_op jit(solution)/shard_map/reduce_scatter | solution.py:64
  92.0 4.5 copy-start.10
  92.0 4.5 copy-start.15
  97.7 164.5 %reduce-scatter.13.cloned.1.call-start = ((), (), s32[]{:S(2)}) async-start(), calls=%async_computation.12 | async-start | bytes 1114112 | tf_op jit(solution)/shard_map/reduce_scatter | solution.py:61
  101.2 210.3 %all-gather.6.cloned.1.call-start = ((), (), s32[]{:S(2)}) async-start(), calls=%async_computation.13 | async-start | bytes 1114112 | tf_op jit(solution)/shard_map/all_gather | solution.py:80
  264.3 127.3 %all-reduce.6.cloned.1.call-start = ((), (), s32[]{:S(2)}) async-start(), calls=%async_computation.14 | async-start | bytes 2097152 | tf_op jit(solution)/shard_map/psum | solution.py:84
  315.7 160.1 %reduce-scatter.15.cloned.1.call-start = ((), (), s32[]{:S(2)}) async-start(), calls=%async_computation.15 | async-start | bytes 278528 | tf_op jit(solution)/shard_map/reduce_scatter | solution.py:64
  393.6 2.7 collective-permute-start
  399.2 158.4 %reduce-scatter.17.cloned.1.call-start = ((), (), s32[]{:S(2)}) async-start(), calls=%async_computation.16 | async-start | bytes 1114112 | tf_op jit(solution)/shard_map/reduce_scatter | solution.py:61
  401.5 205.4 %all-gather.8.cloned.1.call-start = ((), (), s32[]{:S(2)}) async-start(), calls=%async_computation.17 | async-start | bytes 1114112 | tf_op jit(solution)/shard_map/all_gather | solution.py:80
  559.6 127.3 %all-reduce.8.cloned.1.call-start = ((), (), s32[]{:S(2)}) async-start(), calls=%async_computation.18 | async-start | bytes 2097152 | tf_op jit(solution)/shard_map/psum | solution.py:84
  611.0 160.9 %reduce-scatter.19.cloned.1.call-start = ((), (), s32[]{:S(2)}) async-start(), calls=%async_computation.19 | async-start | bytes 278528 | tf_op jit(solution)/shard_map/reduce_scatter | solution.py:64
  688.5 5.6 copy-start.12
  688.6 2.9 collective-permute-start.1
  695.3 158.5 %reduce-scatter.21.cloned.1.call-start = ((), (), s32[]{:S(2)}) async-start(), calls=%async_computation.20 | async-start | bytes 1114112 | tf_op jit(solution)/shard_map/reduce_scatter | solution.py:61
  698.8 204.3 %all-gather.10.cloned.1.call-start = ((), (), s32[]{:S(2)}) async-start(), calls=%async_computation.21 | async-start | bytes 1114112 | tf_op jit(solution)/shard_map/all_gather | solution.py:80
  855.8 127.4 %all-reduce.10.cloned.1.call-start = ((), (), s32[]{:S(2)}) async-start(), calls=%async_computation.22 | async-start | bytes 2097152 | tf_op jit(solution)/shard_map/psum | solution.py:84
  907.3 162.1 %reduce-scatter.23.cloned.1.call-start = ((), (), s32[]{:S(2)}) async-start(), calls=%async_computation.23 | async-start | bytes 278528 | tf_op jit(solution)/shard_map/reduce_scatter | solution.py:64
  985.2 6.4 copy-start.13
  985.2 2.7 collective-permute-start.2
  992.8 158.4 %reduce-scatter.25.cloned.1.call-start = ((), (), s32[]{:S(2)}) async-start(), calls=%async_computation.24 | async-start | bytes 1114112 | tf_op jit(solution)/shard_map/reduce_scatter | solution.py:61
  996.3 204.0 %all-gather.12.cloned.1.call-start = ((), (), s32[]{:S(2)}) async-start(), calls=%async_computation.25 | async-start | bytes 1114112 | tf_op jit(solution)/shard_map/all_gather | solution.py:80
  1153.2 127.2 %all-reduce.12.cloned.1.call-start = ((), (), s32[]{:S(2)}) async-start(), calls=%async_computation.26 | async-start | bytes 2097152 | tf_op jit(solution)/shard_map/psum | solution.py:84
  1204.5 160.4 %reduce-scatter.27.cloned.1.call-start = ((), (), s32[]{:S(2)}) async-start(), calls=%async_computation.27 | async-start | bytes 278528 | tf_op jit(solution)/shard_map/reduce_scatter | solution.py:64
  1280.4 6.7 copy-start.14
  1283.4 2.7 collective-permute-start.3
  1288.2 158.4 %reduce-scatter.29.cloned.1.call-start = ((), (), s32[]{:S(2)}) async-start(), calls=%async_computation.28 | async-start | bytes 1114112 | tf_op jit(solution)/shard_map/reduce_scatter | solution.py:61
  1290.6 205.4 %all-gather.14.cloned.1.call-start = ((), (), s32[]{:S(2)}) async-start(), calls=%async_computation.29 | async-start | bytes 1114112 | tf_op jit(solution)/shard_map/all_gather | solution.py:80
  1448.7 127.4 %all-reduce.14.cloned.1.call-start = ((), (), s32[]{:S(2)}) async-start(), calls=%async_computation.30 | async-start | bytes 2097152 | tf_op jit(solution)/shard_map/psum | solution.py:84
  (9 other events, 14.9 us)
Sparse Core Ops, SparseCore 0:
  97.8 82.3 reduce-scatter.10
  183.7 78.5 reduce-scatter.12
  264.7 46.8 all-gather.5
  315.8 75.7 all-reduce.5
  399.3 76.4 reduce-scatter.14
  479.2 78.2 reduce-scatter.16
  560.0 46.8 all-gather.7
  611.1 75.7 all-reduce.7
  695.4 76.4 reduce-scatter.18
  775.3 78.4 reduce-scatter.20
  856.2 46.8 all-gather.9
  907.4 75.7 all-reduce.9
  992.9 76.4 reduce-scatter.22
  1072.7 78.3 reduce-scatter.24
  1153.4 46.8 all-gather.11
  1204.6 75.7 all-reduce.11
  1288.4 76.4 reduce-scatter.26
  1368.2 78.4 reduce-scatter.28
  1449.1 46.8 all-gather.13
  1500.3 75.7 all-reduce.13
where the time goes:
time: 1590 us
  waiting for transfers between devices  1270 us (80%)
  blocking collectives  185 us (12%)
  matrix products  48.2 us (3%)
  local copies, waits for them, and re-layouts  29.8 us (2%)
  other arithmetic  26 us (2%)
    reduce_scatter x5, waiting for transfers between devices, section_layer(): lax.psum_scatter(query_terms.astype(jnp.bfloat16), 'dp', scatter_dimensio...  405 us
    psum x5, waiting for transfers between devices, section_layer(): lax.psum(head_terms.astype(jnp.bfloat16), 'tensor').astype(jnp.float32)  379 us
    all_gather x5, waiting for transfers between devices, section_layer(): lax.all_gather(attended_rows, 'dp', axis=0, tiled=True)  236 us
    psum x5, blocking collectives, section_layer(): all_squares = lax.psum(square_terms, 'dp')  185 us
    reduce_scatter x5, waiting for transfers between devices, section_layer(): lax.psum_scatter(keyval_terms.astype(jnp.bfloat16), 'dp', scatter_dimensi...  185 us
    all_to_all x1, waiting for transfers between devices, on_device(): lax.all_to_all(tokens, 'dp', split_axis=1, concat_axis=0, tiled=True)  59.1 us
  transfers between devices with their start and end apart: 25, of which 25 were waited for; matrix products, arithmetic and copies ran while one was open for 1% of the time, Pallas kernels for 0%

commit v1 on v0

--- a/solution.py
+++ b/solution.py
@@ -45,6 +45,18 @@
 def section_layer(
     hidden, sentence_segment_rows, gain_row, query_weight, key_value_matrix, out_weight
 ):
+
+    def report_zones(arr_in, named_axis):
+        return jnp.concatenate(
+            lax.all_to_all(
+                jnp.stack([arr_in] * lax.axis_size(named_axis), 0),
+                axis_name=named_axis,
+                split_axis=0,
+                concat_axis=0,
+            ),
+            0,
+        )
+
     slice_width = hidden.shape[1]
     own_rows = sentence_segment_rows.shape[0]
     own_start = lax.axis_index("dp") * own_rows
@@ -77,9 +89,7 @@
         query_rows, key_value_rows, sentence_segment_rows, QUERY_HEADS // KEYVALUE_HEADS
     )
     head_terms = jnp.dot(
-        lax.all_gather(attended_rows, "dp", axis=0, tiled=True),
-        out_weight,
-        preferred_element_type=jnp.float32,
+        report_zones(attended_rows, "dp"), out_weight, preferred_element_type=jnp.float32
     )
     head_total = lax.psum(head_terms.astype(jnp.bfloat16), "tensor").astype(jnp.float32)
     return (widened + head_total).astype(jnp.bfloat16)

time: 1590 us -> 1430 us (0.90)
  waiting for transfers between devices: 1270 us -> 1030 us
  blocking collectives: 185 us -> 283 us
    all_gather x5 -> x0, waiting for transfers between devices: 236 us -> none  [section_layer(): lax.all_gather(attended_rows, 'dp', axis=0, tiled=True)]
    all_to_all x0 -> x5, blocking collectives: none -> 97.8 us  [report_zones(): lax.all_to_all(jnp.stack([arr_in] * lax.axis_size(named_axis), 0), axis_n...]
  transfers between devices with their start and end apart: 25 -> 20, of which waited for: 25 -> 20; matrix products, arithmetic and copies ran while one was open for 1% -> 2% of each run, Pallas kernels for 0% -> 0%
where the time goes in v1:
time: 1430 us
  waiting for transfers between devices  1030 us (72%)
  blocking collectives  283 us (20%)
  matrix products  38.7 us (3%)
  local copies, waits for them, and re-layouts  27.3 us (2%)
  other arithmetic  26 us (2%)
    reduce_scatter x5, waiting for transfers between devices, section_layer(): lax.psum_scatter(query_terms.astype(jnp.bfloat16), 'dp', scatter_dimensio...  405 us
    psum x5, waiting for transfers between devices, section_layer(): lax.psum(head_terms.astype(jnp.bfloat16), 'tensor').astype(jnp.float32)  373 us
    psum x5, blocking collectives, section_layer(): all_squares = lax.psum(square_terms, 'dp')  185 us
    reduce_scatter x5, waiting for transfers between devices, section_layer(): lax.psum_scatter(keyval_terms.astype(jnp.bfloat16), 'dp', scatter_dimensi...  185 us
    all_to_all x5, blocking collectives, report_zones(): lax.all_to_all(jnp.stack([arr_in] * lax.axis_size(named_axis), 0), axis_n...  97.8 us
    all_to_all x1, waiting for transfers between devices, on_device(): lax.all_to_all(tokens, 'dp', split_axis=1, concat_axis=0, tiled=True)  59.1 us
  transfers between devices with their start and end apart: 20, of which 20 were waited for; matrix products, arithmetic and copies ran while one was open for 2% of the time, Pallas kernels for 0%

profile of v1, /device:TPU:2, one launch (start us, length us, event | category | flops | bytes accessed | tf_op | source)
XLA Modules:
  0.0 1430.6 jit_solution(15268801265714493362)
XLA Ops:
  6.5 4.9 copy.87
  11.5 7.6 all-to-all-start
  19.2 59.1 %all-to-all-done = bf16[128,16,1024]{2,0,1:T(8,128)(2,1)} async-done(((bf16[128,16,1024]{2,0,1:T(8,128)(2,1)}), bf16[128,16,1024]{2,0,1:T(8,128)(2,1)}, u32[]{:S(2)}, u32[]{:S(2)}) %all-to-all-start) | async-done | bytes 4194336 | tf_op jit(solution)/shard_map/all_to_all | solution.py:99
  78.3 13.7 gather_fusion
  97.7 3.5 fusion.35
  103.8 39.7 %psum.70 = f32[512]{0:T(512)S(1)} all-reduce(f32[512]{0:T(512)S(1)} %fusion.1), channel_id=1, replica_groups=mesh['dp'=16,'section'=2,'tensor'=8] {'dp'}, use_global_device_ids=true, to_apply=%region_2.3 | all-reduce | flops 512 | bytes 4096 | tf_op jit(solution)/shard_map/psum | solution.py:70
  143.6 36.5 %reduce-scatter.11.cloned.1.call-done = bf16[32,256]{1,0:T(8,128)(2,1)} async-done(((bf16[512,256]{1,0:T(8,128)(2,1)}), bf16[32,256]{1,0:T(8,128)(2,1)}) %reduce-scatter.11.cloned.1.call-update) | async-done | bytes 16400 | tf_op jit(solution)/shard_map/reduce_scatter | solution.py:76
  180.9 81.1 %reduce-scatter.13.cloned.1.call-done = bf16[32,1024]{1,0:T(8,128)(2,1)} async-done(((bf16[512,1024]{1,0:T(8,128)(2,1)}), bf16[32,1024]{1,0:T(8,128)(2,1)}) %reduce-scatter.13.cloned.1.call-update) | async-done | bytes 65552 | tf_op jit(solution)/shard_map/reduce_scatter | solution.py:73
  263.6 19.6 %all_to_all.44 = bf16[16,32,1024]{2,1,0:T(8,128)(2,1)S(1)} all-to-all(bf16[16,32,1024]{2,1,0:T(8,128)(2,1)S(1)} %stack.15), channel_id=1, replica_groups=mesh['dp'=16,'section'=2,'tensor'=8] {'dp'}, dimensions={0} | all-to-all | bytes 2097152 | tf_op jit(solution)/shard_map/all_to_all | solution.py:51
  285.5 74.5 %all-reduce.6.cloned.1.call-done = bf16[512,1024]{1,0:T(8,128)(2,1)} async-done(((bf16[512,1024]{1,0:T(8,128)(2,1)}), bf16[512,1024]{1,0:T(8,128)(2,1)}) %all-reduce.6.cloned.1.call-update) | async-done | bytes 1048592 | tf_op jit(solution)/shard_map/psum | solution.py:94
  370.0 36.4 %psum.72 = f32[512]{0:T(512)S(1)} all-reduce(f32[512]{0:T(512)S(1)} %get-tuple-element.9), channel_id=1, replica_groups=mesh['dp'=16,'section'=2,'tensor'=8] {'dp'}, use_global_device_ids=true, to_apply=%region_8.9 | all-reduce | flops 512 | bytes 4096 | tf_op jit(solution)/shard_map/psum | solution.py:70
  406.5 37.8 %reduce-scatter.15.cloned.1.call-done = bf16[32,256]{1,0:T(8,128)(2,1)} async-done(((bf16[512,256]{1,0:T(8,128)(2,1)}), bf16[32,256]{1,0:T(8,128)(2,1)}) %reduce-scatter.15.cloned.1.call-update) | async-done | bytes 16400 | tf_op jit(solution)/shard_map/reduce_scatter | solution.py:76
  445.0 81.0 %reduce-scatter.17.cloned.1.call-done = bf16[32,1024]{1,0:T(8,128)(2,1)} async-done(((bf16[512,1024]{1,0:T(8,128)(2,1)}), bf16[32,1024]{1,0:T(8,128)(2,1)}) %reduce-scatter.17.cloned.1.call-update) | async-done | bytes 65552 | tf_op jit(solution)/shard_map/reduce_scatter | solution.py:73
  527.6 19.6 %all_to_all.45 = bf16[16,32,1024]{2,1,0:T(8,128)(2,1)S(1)} all-to-all(bf16[16,32,1024]{2,1,0:T(8,128)(2,1)S(1)} %stack.16), channel_id=1, replica_groups=mesh['dp'=16,'section'=2,'tensor'=8] {'dp'}, dimensions={0} | all-to-all | bytes 2097152 | tf_op jit(solution)/shard_map/all_to_all | solution.py:51
  549.4 74.6 %all-reduce.8.cloned.1.call-done = bf16[512,1024]{1,0:T(8,128)(2,1)} async-done(((bf16[512,1024]{1,0:T(8,128)(2,1)}), bf16[512,1024]{1,0:T(8,128)(2,1)}) %all-reduce.8.cloned.1.call-update) | async-done | bytes 1048592 | tf_op jit(solution)/shard_map/psum | solution.py:94
  632.5 3.5 fusion.41
  636.1 36.4 %psum.74 = f32[512]{0:T(512)S(1)} all-reduce(f32[512]{0:T(512)S(1)} %get-tuple-element.7), channel_id=1, replica_groups=mesh['dp'=16,'section'=2,'tensor'=8] {'dp'}, use_global_device_ids=true, to_apply=%region_14.15 | all-reduce | flops 512 | bytes 4096 | tf_op jit(solution)/shard_map/psum | solution.py:70
  672.6 36.5 %reduce-scatter.19.cloned.1.call-done = bf16[32,256]{1,0:T(8,128)(2,1)} async-done(((bf16[512,256]{1,0:T(8,128)(2,1)}), bf16[32,256]{1,0:T(8,128)(2,1)}) %reduce-scatter.19.cloned.1.call-update) | async-done | bytes 16400 | tf_op jit(solution)/shard_map/reduce_scatter | solution.py:76
  709.9 81.2 %reduce-scatter.21.cloned.1.call-done = bf16[32,1024]{1,0:T(8,128)(2,1)} async-done(((bf16[512,1024]{1,0:T(8,128)(2,1)}), bf16[32,1024]{1,0:T(8,128)(2,1)}) %reduce-scatter.21.cloned.1.call-update) | async-done | bytes 65552 | tf_op jit(solution)/shard_map/reduce_scatter | solution.py:73
  792.6 19.6 %all_to_all.46 = bf16[16,32,1024]{2,1,0:T(8,128)(2,1)S(1)} all-to-all(bf16[16,32,1024]{2,1,0:T(8,128)(2,1)S(1)} %stack.17), channel_id=1, replica_groups=mesh['dp'=16,'section'=2,'tensor'=8] {'dp'}, dimensions={0} | all-to-all | bytes 2097152 | tf_op jit(solution)/shard_map/all_to_all | solution.py:51
  814.5 74.6 %all-reduce.10.cloned.1.call-done = bf16[512,1024]{1,0:T(8,128)(2,1)} async-done(((bf16[512,1024]{1,0:T(8,128)(2,1)}), bf16[512,1024]{1,0:T(8,128)(2,1)}) %all-reduce.10.cloned.1.call-update) | async-done | bytes 1048592 | tf_op jit(solution)/shard_map/psum | solution.py:94
  898.8 3.5 fusion.44
  902.4 36.4 %psum.76 = f32[512]{0:T(512)S(1)} all-reduce(f32[512]{0:T(512)S(1)} %get-tuple-element.5), channel_id=1, replica_groups=mesh['dp'=16,'section'=2,'tensor'=8] {'dp'}, use_global_device_ids=true, to_apply=%region_20.21 | all-reduce | flops 512 | bytes 4096 | tf_op jit(solution)/shard_map/psum | solution.py:70
  938.9 36.5 %reduce-scatter.23.cloned.1.call-done = bf16[32,256]{1,0:T(8,128)(2,1)} async-done(((bf16[512,256]{1,0:T(8,128)(2,1)}), bf16[32,256]{1,0:T(8,128)(2,1)}) %reduce-scatter.23.cloned.1.call-update) | async-done | bytes 16400 | tf_op jit(solution)/shard_map/reduce_scatter | solution.py:76
  976.2 81.2 %reduce-scatter.25.cloned.1.call-done = bf16[32,1024]{1,0:T(8,128)(2,1)} async-done(((bf16[512,1024]{1,0:T(8,128)(2,1)}), bf16[32,1024]{1,0:T(8,128)(2,1)}) %reduce-scatter.25.cloned.1.call-update) | async-done | bytes 65552 | tf_op jit(solution)/shard_map/reduce_scatter | solution.py:73
  1058.9 19.6 %all_to_all.47 = bf16[16,32,1024]{2,1,0:T(8,128)(2,1)S(1)} all-to-all(bf16[16,32,1024]{2,1,0:T(8,128)(2,1)S(1)} %stack.18), channel_id=1, replica_groups=mesh['dp'=16,'section'=2,'tensor'=8] {'dp'}, dimensions={0} | all-to-all | bytes 2097152 | tf_op jit(solution)/shard_map/all_to_all | solution.py:51
  1080.8 74.6 %all-reduce.12.cloned.1.call-done = bf16[512,1024]{1,0:T(8,128)(2,1)} async-done(((bf16[512,1024]{1,0:T(8,128)(2,1)}), bf16[512,1024]{1,0:T(8,128)(2,1)}) %all-reduce.12.cloned.1.call-update) | async-done | bytes 1048592 | tf_op jit(solution)/shard_map/psum | solution.py:94
  1166.0 36.4 %psum.78 = f32[512]{0:T(512)S(1)} all-reduce(f32[512]{0:T(512)S(1)} %fusion.13), channel_id=1, replica_groups=mesh['dp'=16,'section'=2,'tensor'=8] {'dp'}, use_global_device_ids=true, to_apply=%region_26.27 | all-reduce | flops 512 | bytes 4096 | tf_op jit(solution)/shard_map/psum | solution.py:70
  1202.5 37.4 %reduce-scatter.27.cloned.1.call-done = bf16[32,256]{1,0:T(8,128)(2,1)} async-done(((bf16[512,256]{1,0:T(8,128)(2,1)}), bf16[32,256]{1,0:T(8,128)(2,1)}) %reduce-scatter.27.cloned.1.call-update) | async-done | bytes 16400 | tf_op jit(solution)/shard_map/reduce_scatter | solution.py:76
  1240.7 80.9 %reduce-scatter.29.cloned.1.call-done = bf16[32,1024]{1,0:T(8,128)(2,1)} async-done(((bf16[512,1024]{1,0:T(8,128)(2,1)}), bf16[32,1024]{1,0:T(8,128)(2,1)}) %reduce-scatter.29.cloned.1.call-update) | async-done | bytes 65552 | tf_op jit(solution)/shard_map/reduce_scatter | solution.py:73
  1323.2 19.6 %all_to_all.48 = bf16[16,32,1024]{2,1,0:T(8,128)(2,1)S(1)} all-to-all(bf16[16,32,1024]{2,1,0:T(8,128)(2,1)S(1)} %stack.19), channel_id=1, replica_groups=mesh['dp'=16,'section'=2,'tensor'=8] {'dp'}, dimensions={0} | all-to-all | bytes 2097152 | tf_op jit(solution)/shard_map/all_to_all | solution.py:51
  1345.1 74.6 %all-reduce.14.cloned.1.call-done = bf16[512,1024]{1,0:T(8,128)(2,1)} async-done(((bf16[512,1024]{1,0:T(8,128)(2,1)}), bf16[512,1024]{1,0:T(8,128)(2,1)}) %all-reduce.14.cloned.1.call-update) | async-done | bytes 1048592 | tf_op jit(solution)/shard_map/psum | solution.py:94
  (147 shorter events, 74.8 us)
Async XLA Ops:
  6.5 91.2 %copy-start = (bf16[1,1024,1024]{2,1,0:T(8,128)(2,1)S(1)}, bf16[1,1024,1024]{2,1,0:T(8,128)(2,1)}, u32[]{:S(2)}) copy-start(bf16[1,1024,1024]{2,1,0:T(8,128)(2,1)} %param.11) | copy-start | bytes 6291460
  11.5 7.7 copy-start.9
  11.5 66.8 %all-to-all-start = ((bf16[128,16,1024]{2,0,1:T(8,128)(2,1)}), bf16[128,16,1024]{2,0,1:T(8,128)(2,1)}, u32[]{:S(2)}, u32[]{:S(2)}) async-start(bf16[128,16,1024]{2,0,1:T(8,128)(2,1)} %bitcast.271), calls=%async_computation | async-start | bytes 8388608 | tf_op jit(solution)/shard_map/all_to_all | solution.py:99
  19.1 161.0 %reduce-scatter.11.cloned.1.call-start = ((), (), s32[]{:S(2)}) async-start(), calls=%async_computation.16 | async-start | bytes 278528 | tf_op jit(solution)/shard_map/reduce_scatter | solution.py:76
  92.0 4.5 copy-start.15
  92.0 4.5 copy-start.20
  97.7 164.4 %reduce-scatter.13.cloned.1.call-start = ((), (), s32[]{:S(2)}) async-start(), calls=%async_computation.17 | async-start | bytes 1114112 | tf_op jit(solution)/shard_map/reduce_scatter | solution.py:73
  101.2 258.8 %all-reduce.6.cloned.1.call-start = ((), (), s32[]{:S(2)}) async-start(), calls=%async_computation.18 | async-start | bytes 2097152 | tf_op jit(solution)/shard_map/psum | solution.py:94
  263.2 20.0 %copy-start.10 = (bf16[1,1024,1024]{2,1,0:T(8,128)(2,1)S(1)}, bf16[1,1024,1024]{2,1,0:T(8,128)(2,1)}, u32[]{:S(2)}) copy-start(bf16[1,1024,1024]{2,1,0:T(8,128)(2,1)} %param.13) | copy-start | bytes 6291460
  285.4 158.8 %reduce-scatter.15.cloned.1.call-start = ((), (), s32[]{:S(2)}) async-start(), calls=%async_computation.19 | async-start | bytes 278528 | tf_op jit(solution)/shard_map/reduce_scatter | solution.py:76
  362.0 2.7 collective-permute-start
  367.6 158.4 %reduce-scatter.17.cloned.1.call-start = ((), (), s32[]{:S(2)}) async-start(), calls=%async_computation.20 | async-start | bytes 1114112 | tf_op jit(solution)/shard_map/reduce_scatter | solution.py:73
  369.9 254.2 %all-reduce.8.cloned.1.call-start = ((), (), s32[]{:S(2)}) async-start(), calls=%async_computation.21 | async-start | bytes 2097152 | tf_op jit(solution)/shard_map/psum | solution.py:94
  527.2 20.0 %copy-start.11 = (bf16[1,1024,1024]{2,1,0:T(8,128)(2,1)S(1)}, bf16[1,1024,1024]{2,1,0:T(8,128)(2,1)}, u32[]{:S(2)}) copy-start(bf16[1,1024,1024]{2,1,0:T(8,128)(2,1)} %param.13) | copy-start | bytes 6291460
  549.4 159.7 %reduce-scatter.19.cloned.1.call-start = ((), (), s32[]{:S(2)}) async-start(), calls=%async_computation.22 | async-start | bytes 278528 | tf_op jit(solution)/shard_map/reduce_scatter | solution.py:76
  625.7 5.6 copy-start.17
  625.7 2.9 collective-permute-start.1
  632.5 158.6 %reduce-scatter.21.cloned.1.call-start = ((), (), s32[]{:S(2)}) async-start(), calls=%async_computation.23 | async-start | bytes 1114112 | tf_op jit(solution)/shard_map/reduce_scatter | solution.py:73
  636.0 253.2 %all-reduce.10.cloned.1.call-start = ((), (), s32[]{:S(2)}) async-start(), calls=%async_computation.24 | async-start | bytes 2097152 | tf_op jit(solution)/shard_map/psum | solution.py:94
  792.2 20.0 %copy-start.12 = (bf16[1,1024,1024]{2,1,0:T(8,128)(2,1)S(1)}, bf16[1,1024,1024]{2,1,0:T(8,128)(2,1)}, u32[]{:S(2)}) copy-start(bf16[1,1024,1024]{2,1,0:T(8,128)(2,1)} %param.13) | copy-start | bytes 6291460
  814.5 160.9 %reduce-scatter.23.cloned.1.call-start = ((), (), s32[]{:S(2)}) async-start(), calls=%async_computation.25 | async-start | bytes 278528 | tf_op jit(solution)/shard_map/reduce_scatter | solution.py:76
  891.1 6.4 copy-start.18
  891.1 2.7 collective-permute-start.2
  898.7 158.6 %reduce-scatter.25.cloned.1.call-start = ((), (), s32[]{:S(2)}) async-start(), calls=%async_computation.26 | async-start | bytes 1114112 | tf_op jit(solution)/shard_map/reduce_scatter | solution.py:73
  902.3 253.1 %all-reduce.12.cloned.1.call-start = ((), (), s32[]{:S(2)}) async-start(), calls=%async_computation.27 | async-start | bytes 2097152 | tf_op jit(solution)/shard_map/psum | solution.py:94
  1058.5 20.0 %copy-start.13 = (bf16[1,1024,1024]{2,1,0:T(8,128)(2,1)S(1)}, bf16[1,1024,1024]{2,1,0:T(8,128)(2,1)}, u32[]{:S(2)}) copy-start(bf16[1,1024,1024]{2,1,0:T(8,128)(2,1)} %param.13) | copy-start | bytes 6291460
  1080.7 159.2 %reduce-scatter.27.cloned.1.call-start = ((), (), s32[]{:S(2)}) async-start(), calls=%async_computation.28 | async-start | bytes 278528 | tf_op jit(solution)/shard_map/reduce_scatter | solution.py:76
  1155.4 6.7 copy-start.19
  1158.4 2.7 collective-permute-start.3
  1163.2 158.4 %reduce-scatter.29.cloned.1.call-start = ((), (), s32[]{:S(2)}) async-start(), calls=%async_computation.29 | async-start | bytes 1114112 | tf_op jit(solution)/shard_map/reduce_scatter | solution.py:73
  1165.6 254.2 %all-reduce.14.cloned.1.call-start = ((), (), s32[]{:S(2)}) async-start(), calls=%async_computation.30 | async-start | bytes 2097152 | tf_op jit(solution)/shard_map/psum | solution.py:94
  1322.8 20.0 %copy-start.14 = (bf16[1,1024,1024]{2,1,0:T(8,128)(2,1)S(1)}, bf16[1,1024,1024]{2,1,0:T(8,128)(2,1)}, u32[]{:S(2)}) copy-start(bf16[1,1024,1024]{2,1,0:T(8,128)(2,1)} %param.13) | copy-start | bytes 6291460
  (9 other events, 15.0 us)
Sparse Core Ops, SparseCore 0:
  97.8 82.2 reduce-scatter.10
  183.6 78.3 reduce-scatter.12
  285.5 74.4 all-reduce.5
  367.7 76.4 reduce-scatter.14
  447.6 78.3 reduce-scatter.16
  549.5 74.4 all-reduce.7
  632.6 76.4 reduce-scatter.18
  712.6 78.4 reduce-scatter.20
  814.6 74.5 all-reduce.9
  898.8 76.4 reduce-scatter.22
  978.9 78.4 reduce-scatter.24
  1080.9 74.4 all-reduce.11
  1163.4 76.5 reduce-scatter.26
  1243.3 78.3 reduce-scatter.28
  1345.2 74.4 all-reduce.13
